TPU v7x, 32 devices: a whole 2x2x4 slice. The times are simulated.
32 devices in a mesh: expert: 8 (over z, x), rep: 4 (over y, core).
Axes of the slice: x: 2, y: 2, z: 4, core: 2. Of those that a mesh axis runs over, the one named last changes fastest.
Arguments:
- tokens: bfloat16 [4, 2048, 2, 2048], P('rep', 'expert'), may hold values from -6 to 6
- expert_ids: int32 [4, 2048, 2, 2], P('rep', 'expert'), may hold values from 0 to 15, all different within a row; in each aligned block of 512 rows (0 to 511, 512 to 1023, ..., all dimensions but the last counted through in order) at most 80 rows name the same one
- gate_probs: float32 [4, 2048, 2, 2], P('rep', 'expert'), may hold values from 0.1 to 1
- norm_gain: float32 [2048], replicated, may hold values from 0.25 to 1.75
- expert_gate: bfloat16 [16, 2048, 1408], P('expert', None, 'rep'), may hold values from -0.125 to 0.125
- expert_up: bfloat16 [16, 2048, 1408], P('expert', None, 'rep'), may hold values from -0.125 to 0.125
- expert_down: bfloat16 [16, 1408, 2048], P('expert', 'rep'), may hold values from -0.15625 to 0.15625
- teacher_gain: float32 [2048], replicated, may hold values from 0.25 to 1.75
- teacher_qkv: bfloat16 [2048, 3, 16, 128], P(None, None, 'rep')
- qk_gain: float32 [2, 16, 128], P(None, 'rep'), may hold values from 0.5 to 7.5
- teacher_out: bfloat16 [16, 128, 2048], P('rep'), may hold values from -0.125 to 0.125
- critic_in: bfloat16 [2048, 1024], replicated, may hold values from -0.125 to 0.125
- critic_out: float32 [1024], replicated, may hold values from -0.1875 to 0.1875
Outputs:
- teacher_features: bfloat16 [4, 2048, 2, 2048], P('rep', 'expert')
- critic_logits: float32 [4, 2048, 2], P('rep', 'expert')
Inputs may be any that keep to these rules, and one draw needn't show every extreme that they name: `expert_ids`: the 512 rows of one device name one expert at most 80 times in all, and some device reaches 80; the two experts of a token differ.
All inputs are finite; a program needn't handle non-finite values.
Results may differ from a plain program's by a relative error of at most 0.033.
Values may be sent and summed in bfloat16 or wider, within the bound.
No kernel may reach another device: no remote copies, remote signals or barrier semaphores. Data moves between devices by JAX's collectives and lax.ppermute only.
A program may use at most 192 MiB of HBM per device.

v0:
```python
import jax
import jax.numpy as jnp
from jax import lax
from jax.sharding import PartitionSpec as P


def norm_rows(values, gain):
    return values * lax.rsqrt(jnp.mean(values * values, axis=-1, keepdims=True) + 1e-06) * gain


def slot_numbers(chosen, count):
    onehot = (chosen[..., None] == jnp.arange(count, dtype=jnp.int32)).astype(jnp.int32)
    before = jnp.cumsum(onehot, axis=-2) - onehot
    return jnp.sum(before * onehot, axis=-1)


def local(
    tokens,
    expert_ids,
    gate_probs,
    norm_gain,
    expert_gate,
    expert_up,
    expert_down,
    teacher_gain,
    teacher_qkv,
    qk_gain,
    teacher_out,
    critic_in,
    critic_out,
):
    seq_dev = tokens.shape[1]
    images = tokens.shape[2]
    width = tokens.shape[3]
    tok_count = seq_dev * images
    n_owner = lax.axis_size("expert")
    n_replica = lax.axis_size("rep")
    exp_local = expert_gate.shape[0]
    expert_total = exp_local * n_owner
    capacity = max(2, tok_count * 10 // (4 * expert_total))
    gate_full = lax.all_gather(expert_gate, "rep", axis=2, tiled=True)
    up_full = lax.all_gather(expert_up, "rep", axis=2, tiled=True)
    down_full = lax.all_gather(expert_down, "rep", axis=1, tiled=True)
    qkv_full = lax.all_gather(teacher_qkv, "rep", axis=2, tiled=True)
    qk_gain_full = lax.all_gather(qk_gain, "rep", axis=1, tiled=True)
    out_full = lax.all_gather(teacher_out, "rep", axis=0, tiled=True)
    residual = tokens.reshape(tok_count, width).astype(jnp.float32)
    normed = norm_rows(residual, norm_gain).astype(jnp.bfloat16)
    chosen = expert_ids.reshape(2 * tok_count)
    slot_index = slot_numbers(chosen, expert_total)
    gate_value = gate_probs.reshape(2 * tok_count)
    target = chosen * capacity + slot_index
    token_of = jnp.arange(2 * tok_count, dtype=jnp.int32) // 2
    owner_token = jnp.zeros((expert_total * capacity,), jnp.int32).at[target].set(token_of)
    filled = jnp.zeros((expert_total * capacity,), jnp.bool_).at[target].set(True)
    outgoing = jnp.where(
        filled[:, None], jnp.take(normed, owner_token, axis=0), jnp.zeros((), jnp.bfloat16)
    )
    outgoing = outgoing.reshape(n_owner, exp_local * capacity, width)
    arrived = lax.all_to_all(outgoing, "expert", split_axis=0, concat_axis=0, tiled=True)
    arrived = arrived.reshape(n_owner, exp_local, capacity, width)
    gate_part = jnp.einsum("sjcd,jdf->sjcf", arrived, gate_full, preferred_element_type=jnp.float32)
    up_part = jnp.einsum("sjcd,jdf->sjcf", arrived, up_full, preferred_element_type=jnp.float32)
    hidden = (jax.nn.silu(gate_part) * up_part).astype(jnp.bfloat16)
    ff_total = hidden.shape[-1]
    ff_part = ff_total // n_replica
    produced = jnp.zeros(arrived.shape, jnp.float32)
    for part in range(n_replica):
        low = part * ff_part
        produced = produced + jnp.einsum(
            "sjcf,jfd->sjcd",
            hidden[..., low : low + ff_part],
            down_full[:, low : low + ff_part],
            preferred_element_type=jnp.float32,
        ).astype(jnp.bfloat16).astype(jnp.float32)
    results = produced.astype(jnp.bfloat16).reshape(n_owner, exp_local * capacity, width)
    returned = lax.all_to_all(results, "expert", split_axis=0, concat_axis=0, tiled=True).reshape(
        expert_total * capacity, width
    )
    picked = jnp.take(returned, target, axis=0).astype(jnp.float32) * gate_value[:, None]
    combined = picked.reshape(tok_count, 2, width).sum(axis=1)
    mixed = (residual + combined).astype(jnp.bfloat16)
    teacher_in = norm_rows(mixed.astype(jnp.float32), teacher_gain).astype(jnp.bfloat16)
    teacher_in = teacher_in.reshape(seq_dev, images, width)
    heads_all = qkv_full.shape[2]
    head_size = qkv_full.shape[3]
    projected = jnp.einsum(
        "sid,djhe->jihse", teacher_in, qkv_full, preferred_element_type=jnp.float32
    )
    query = norm_rows(projected[0], qk_gain_full[0][:, None, :])
    keyed = norm_rows(projected[1], qk_gain_full[1][:, None, :])
    projected = jnp.stack([query, keyed, projected[2]]).astype(jnp.bfloat16)
    pairs_all = images * heads_all
    grouped = projected.reshape(3, pairs_all, seq_dev, head_size)
    whole = lax.all_to_all(grouped, "expert", split_axis=1, concat_axis=2, tiled=True)
    pairs_local = whole.shape[1]
    seq_len = whole.shape[2]
    block = min(512, seq_len)
    blocks_count = seq_len // block
    key_rows = whole[1]
    value_rows = whole[2]

    def attend(query_block):
        scores = jnp.einsum(
            "pqe,pke->pqk", query_block, key_rows, preferred_element_type=jnp.float32
        ) * head_size ** (-0.5)
        scores = scores - jnp.max(scores, axis=-1, keepdims=True)
        weights = jnp.exp(scores)
        probs = (weights / jnp.sum(weights, axis=-1, keepdims=True)).astype(jnp.bfloat16)
        return jnp.einsum(
            "pqk,pke->pqe", probs, value_rows, preferred_element_type=jnp.float32
        ).astype(jnp.bfloat16)

    query_blocks = (
        whole[0].reshape(pairs_local, blocks_count, block, head_size).transpose(1, 0, 2, 3)
    )
    attended = (
        lax.map(attend, query_blocks).transpose(1, 0, 2, 3).reshape(pairs_local, seq_len, head_size)
    )
    gathered_heads = lax.all_to_all(attended, "expert", split_axis=1, concat_axis=0, tiled=True)
    gathered_heads = gathered_heads.reshape(images, heads_all, seq_dev, head_size)
    heads_part = heads_all // n_replica
    projected_out = jnp.zeros((seq_dev, images, width), jnp.float32)
    for part in range(n_replica):
        low = part * heads_part
        projected_out = projected_out + jnp.einsum(
            "ihse,hed->sid",
            gathered_heads[:, low : low + heads_part],
            out_full[low : low + heads_part],
            preferred_element_type=jnp.float32,
        ).astype(jnp.bfloat16).astype(jnp.float32)
    features = (mixed.reshape(seq_dev, images, width).astype(jnp.float32) + projected_out).astype(
        jnp.bfloat16
    )
    critic_hidden = jax.nn.gelu(
        jnp.dot(features.reshape(tok_count, width), critic_in, preferred_element_type=jnp.float32),
        approximate=True,
    )
    logits = jnp.dot(
        critic_hidden,
        critic_out,
        precision=lax.Precision.HIGHEST,
        preferred_element_type=jnp.float32,
    )
    return (features.reshape(1, seq_dev, images, width), logits.reshape(1, seq_dev, images))


def solution(mesh):
    return jax.shard_map(
        local,
        mesh=mesh,
        in_specs=(
            P("rep", "expert", None, None),
            P("rep", "expert", None, None),
            P("rep", "expert", None, None),
            P(),
            P("expert", None, "rep"),
            P("expert", None, "rep"),
            P("expert", "rep", None),
            P(),
            P(None, None, "rep", None),
            P(None, "rep", None),
            P("rep", None, None),
            P(),
            P(),
        ),
        out_specs=(P("rep", "expert", None, None), P("rep", "expert", None)),
        check_vma=False,
    )
```

profile of v0, /device:TPU:0, one launch (start us, length us, event | category | flops | bytes accessed | tf_op | source)
XLA Modules:
  0.0 909.0 jit_solution(2036090906852341895)
XLA Ops:
  9.4 10.8 %copy.124 = bf16[2048,3,4,128]{0,3,2,1:T(8,128)(2,1)} copy(bf16[2048,3,4,128]{3,2,1,0:T(4,128)(2,1)} %param.23) | data formatting | bytes 12582912 | tf_op args[8]
  63.0 123.0 %all_to_all.40 = bf16[8,160,2048]{2,1,0:T(8,128)(2,1)} all-to-all(bf16[8,160,2048]{2,1,0:T(8,128)(2,1)S(1)} %select_select_fusion), channel_id=1, replica_groups=mesh['expert'=8,'rep'=4] {'expert'}, dimensions={0} | all-to-all | bytes 10485760 | tf_op jit(solution)/shard_map/all_to_all | solution.py:60
  186.0 14.7 %fusion.23 = f32[2,8,80,1408]{3,2,1,0:T(8,128)} fusion(bf16[2,2048,1408]{1,2,0:T(8,128)(2,1)} %all-gather.8.cloned.1.call-done, bf16[8,2,80,2048]{3,2,1,0:T(8,128)(2,1)} %bitcast.207), kind=kOutput, calls=%fused_computation.23 | convolution fusion | flops 7381975040 | bytes 23986176 | tf_op jit(solution)/shard_map/sjcd,jdf->sjcf/dot_general | solution.py:63
  200.7 16.6 %fusion.27 = bf16[8,2,80,1408]{3,2,0,1:T(8,128)(2,1)} fusion(f32[2,8,80,1408]{3,2,1,0:T(8,128)} %fusion.23, bf16[2,2048,1408]{1,2,0:T(8,128)(2,1)} %all-gather.6.cloned.1.call-done, bf16[8,2,80,2048]{3,2,1,0:T(8,128)(2,1)} %bitcast.208), kind=kOutput, calls=%fused_computation.31 | convolution fusion | flops 7392788480 | bytes 27590656 | tf_op jit(solution)/shard_map/sjcd,jdf->sjcf/dot_general | solution.py:62
  217.3 26.6 %all-gather.10.cloned.1.call-done = bf16[2,1408,2048]{2,1,0:T(8,128)(2,1)} async-done(((bf16[2,352,2048]{2,1,0:T(8,128)(2,1)}), bf16[2,1408,2048]{2,1,0:T(8,128)(2,1)}) %all-gather.10.cloned.1.call-update) | async-done | bytes 11534352 | tf_op jit(solution)/shard_map/all_gather | solution.py:43
  288.0 109.6 %all-to-all-done.1 = bf16[8,160,2048]{2,1,0:T(8,128)(2,1)} async-done(((bf16[8,160,2048]{2,1,0:T(8,128)(2,1)}), bf16[8,160,2048]{2,1,0:T(8,128)(2,1)}, u32[]{:S(2)}, u32[]{:S(2)}) %all-to-all-start.1) | async-done | bytes 5242912 | tf_op jit(solution)/shard_map/all_to_all | solution.py:77
  397.7 12.3 %gather_fusion.1 = bf16[1024,2048]{1,0:T(8,128)(2,1)} fusion(bf16[1280,2048]{1,0:T(8,128)(2,1)} %bitcast.25, s32[1024]{0:T(1024)S(1)} %broadcast_clamp_fusion), kind=kCustom, calls=%fused_computation.1 | custom fusion | bytes 8392704 | tf_op jit(solution)/shard_map/jit(_take)/gather | solution.py:80
  417.6 20.7 %multiply_reduce_fusion.1 = f32[512,2048]{1,0:T(8,128)} fusion(bf16[512,2,2048]{2,1,0:T(2,128)(2,1)} %gather.15, pred[512,2]{1,0:T(8,128)(4,1)S(1)} %copy.113, f32[512,2]{1,0:T(8,128)S(1)} %bitcast.215), kind=kLoop, calls=%fused_computation.28 | loop fusion | flops 7340032 | bytes 8393728 | tf_op jit(solution)/shard_map/reduce_sum | solution.py:81
  455.7 26.6 %fusion.36 = f32[3,2,16,256,128]{3,4,2,0,1:T(8,128)} fusion(bf16[2048,3,16,128]{0,3,2,1:T(8,128)(2,1)} %all-gather.12.cloned.1.call-done, f32[2048]{0:T(1024)S(1)} %copy-done.12, f32[256,2]{0,1:T(2,128)S(1)} %add_rsqrt_fusion.2, f32[256,2,2048]{2,1,0:T(2,128)} %reduce_sum.76, bf16[1,256,2,2048]{3,2,1,0:T(2,128)(2,1)S(1)} %copy-done.2), kind=kOutput, calls=%fused_computation.44 | convolution fusion | flops 12892241920 | bytes 44050432 | tf_op jit(solution)/shard_map/sid,djhe->jihse/dot_general | solution.py:87
  516.2 137.0 %all-to-all-done.2 = bf16[3,32,256,128]{3,2,0,1:T(8,128)(2,1)} async-done(((bf16[3,32,256,128]{3,2,0,1:T(8,128)(2,1)}), bf16[3,32,256,128]{3,2,0,1:T(8,128)(2,1)}, u32[]{:S(2)}, u32[]{:S(2)}) %all-to-all-start.2) | async-done | bytes 6291488 | tf_op jit(solution)/shard_map/all_to_all | solution.py:95
  660.1 152.0 %while.10 = (s32[]{:T(128)}, bf16[4,4,512,128]{3,2,0,1:T(8,128)(2,1)}, bf16[4,4,512,128]{3,2,0,1:T(8,128)(2,1)}, bf16[4,2048,128]{2,1,0:T(8,128)(2,1)S(1)}, bf16[4,2048,128]{2,1,0:T(8,128)(2,1)}, /*index=5*/s32[]{:T(128)}) while((s32[]{:T(128)}, bf16[4,4,512,128]{3,2,0,1:T(8,128)(2,1)}, bf16[4,4,512,128]{3,2,0,1:T(8,128)(2,1)}, ...), condition=%wide.region_13.14_spmd, body=%wide.region_10.13_spmd.sunk | while | flops 2185500672 | bytes 72369224 | solution.py:118
  660.2 9.1 %fusion.110 = f32[4,512,2048]{2,1,0:T(8,128)} fusion(bf16[4,2048,128]{2,1,0:T(8,128)(2,1)S(1)} %get-tuple-element.127, bf16[4,4,512,128]{3,2,0,1:T(8,128)(2,1)} %get-tuple-element.126, s32[]{:T(128)} %get-tuple-element.118), kind=kOutput, calls=%fused_computation.14.clone.1 | convolution fusion | flops 1073741824 | bytes 19399168 | tf_op jit(solution)/shard_map/while/body/eval_jaxpr/pqe,pke->pqk/dot_general | solution.py:104
  669.3 14.1 %fusion.111 = f32[4,512]{1,0:T(4,128)S(1)} fusion(f32[4,512,2048]{2,1,0:T(8,128)} %fusion.110), kind=kOutput, calls=%fused_computation.135.clone.1 | output fusion | flops 16779264 | bytes 16785408 | tf_op jit(solution)/shard_map/while/body/eval_jaxpr/sub | solution.py:107
  683.4 14.7 %fusion.112 = bf16[4,4,512,128]{3,2,0,1:T(8,128)(2,1)} fusion(bf16[4,4,512,128]{3,2,0,1:T(8,128)(2,1)} %get-tuple-element.119, s32[]{:T(128)} %get-tuple-element.118, bf16[4,2048,128]{2,1,0:T(8,128)(2,1)} %get-tuple-element.128, f32[4,512]{1,0:T(4,128)S(1)} %fusion.111, f32[4,512,2048]{2,1,0:T(8,128)} %fusion.110), kind=kOutput, calls=%fused_computation.13.clone.1 | convolution fusion | flops 1094979584 | bytes 36184576 | tf_op jit(solution)/shard_map/while/body/eval_jaxpr/pqk,pke->pqe/dot_general | solution.py:110
  698.2 9.1 %fusion.110 = f32[4,512,2048]{2,1,0:T(8,128)} fusion(bf16[4,2048,128]{2,1,0:T(8,128)(2,1)S(1)} %get-tuple-element.127, bf16[4,4,512,128]{3,2,0,1:T(8,128)(2,1)} %get-tuple-element.126, s32[]{:T(128)} %get-tuple-element.118), kind=kOutput, calls=%fused_computation.14.clone.1 | convolution fusion | flops 1073741824 | bytes 19399168 | tf_op jit(solution)/shard_map/while/body/eval_jaxpr/pqe,pke->pqk/dot_general | solution.py:104
  707.3 14.1 %fusion.111 = f32[4,512]{1,0:T(4,128)S(1)} fusion(f32[4,512,2048]{2,1,0:T(8,128)} %fusion.110), kind=kOutput, calls=%fused_computation.135.clone.1 | output fusion | flops 16779264 | bytes 16785408 | tf_op jit(solution)/shard_map/while/body/eval_jaxpr/sub | solution.py:107
  721.4 14.7 %fusion.112 = bf16[4,4,512,128]{3,2,0,1:T(8,128)(2,1)} fusion(bf16[4,4,512,128]{3,2,0,1:T(8,128)(2,1)} %get-tuple-element.119, s32[]{:T(128)} %get-tuple-element.118, bf16[4,2048,128]{2,1,0:T(8,128)(2,1)} %get-tuple-element.128, f32[4,512]{1,0:T(4,128)S(1)} %fusion.111, f32[4,512,2048]{2,1,0:T(8,128)} %fusion.110), kind=kOutput, calls=%fused_computation.13.clone.1 | convolution fusion | flops 1094979584 | bytes 36184576 | tf_op jit(solution)/shard_map/while/body/eval_jaxpr/pqk,pke->pqe/dot_general | solution.py:110
  736.2 9.1 %fusion.110 = f32[4,512,2048]{2,1,0:T(8,128)} fusion(bf16[4,2048,128]{2,1,0:T(8,128)(2,1)S(1)} %get-tuple-element.127, bf16[4,4,512,128]{3,2,0,1:T(8,128)(2,1)} %get-tuple-element.126, s32[]{:T(128)} %get-tuple-element.118), kind=kOutput, calls=%fused_computation.14.clone.1 | convolution fusion | flops 1073741824 | bytes 19399168 | tf_op jit(solution)/shard_map/while/body/eval_jaxpr/pqe,pke->pqk/dot_general | solution.py:104
  745.3 14.1 %fusion.111 = f32[4,512]{1,0:T(4,128)S(1)} fusion(f32[4,512,2048]{2,1,0:T(8,128)} %fusion.110), kind=kOutput, calls=%fused_computation.135.clone.1 | output fusion | flops 16779264 | bytes 16785408 | tf_op jit(solution)/shard_map/while/body/eval_jaxpr/sub | solution.py:107
  759.4 14.7 %fusion.112 = bf16[4,4,512,128]{3,2,0,1:T(8,128)(2,1)} fusion(bf16[4,4,512,128]{3,2,0,1:T(8,128)(2,1)} %get-tuple-element.119, s32[]{:T(128)} %get-tuple-element.118, bf16[4,2048,128]{2,1,0:T(8,128)(2,1)} %get-tuple-element.128, f32[4,512]{1,0:T(4,128)S(1)} %fusion.111, f32[4,512,2048]{2,1,0:T(8,128)} %fusion.110), kind=kOutput, calls=%fused_computation.13.clone.1 | convolution fusion | flops 1094979584 | bytes 36184576 | tf_op jit(solution)/shard_map/while/body/eval_jaxpr/pqk,pke->pqe/dot_general | solution.py:110
  774.2 9.1 %fusion.110 = f32[4,512,2048]{2,1,0:T(8,128)} fusion(bf16[4,2048,128]{2,1,0:T(8,128)(2,1)S(1)} %get-tuple-element.127, bf16[4,4,512,128]{3,2,0,1:T(8,128)(2,1)} %get-tuple-element.126, s32[]{:T(128)} %get-tuple-element.118), kind=kOutput, calls=%fused_computation.14.clone.1 | convolution fusion | flops 1073741824 | bytes 19399168 | tf_op jit(solution)/shard_map/while/body/eval_jaxpr/pqe,pke->pqk/dot_general | solution.py:104
  783.3 14.1 %fusion.111 = f32[4,512]{1,0:T(4,128)S(1)} fusion(f32[4,512,2048]{2,1,0:T(8,128)} %fusion.110), kind=kOutput, calls=%fused_computation.135.clone.1 | output fusion | flops 16779264 | bytes 16785408 | tf_op jit(solution)/shard_map/while/body/eval_jaxpr/sub | solution.py:107
  797.4 14.7 %fusion.112 = bf16[4,4,512,128]{3,2,0,1:T(8,128)(2,1)} fusion(bf16[4,4,512,128]{3,2,0,1:T(8,128)(2,1)} %get-tuple-element.119, s32[]{:T(128)} %get-tuple-element.118, bf16[4,2048,128]{2,1,0:T(8,128)(2,1)} %get-tuple-element.128, f32[4,512]{1,0:T(4,128)S(1)} %fusion.111, f32[4,512,2048]{2,1,0:T(8,128)} %fusion.110), kind=kOutput, calls=%fused_computation.13.clone.1 | convolution fusion | flops 1094979584 | bytes 36184576 | tf_op jit(solution)/shard_map/while/body/eval_jaxpr/pqk,pke->pqe/dot_general | solution.py:110
  815.6 52.2 %all_to_all.41 = bf16[4,2048,128]{2,0,1:T(4,128)(2,1)S(1)} all-to-all(bf16[4,2048,128]{2,0,1:T(4,128)(2,1)S(1)} %copy.135), channel_id=1, replica_groups=mesh['expert'=8,'rep'=4] {'expert'}, dimensions={1} | all-to-all | bytes 4194304 | tf_op jit(solution)/shard_map/all_to_all | solution.py:120
  (128 shorter events, 192.6 us)
Async XLA Ops:
  7.2 888.3 %copy-start = (f32[1024]{0:T(1024)S(1)}, f32[1024]{0:T(1024)}, u32[]{:S(2)}) copy-start(f32[1024]{0:T(1024)} %param.27) | copy-start | bytes 12292
  7.2 178.8 %all-gather.8.cloned.1.call-start = ((), (), s32[]{:S(2)}) async-start(), calls=%async_computation.5 | async-start | bytes 14417920 | tf_op jit(solution)/shard_map/all_gather | solution.py:42
  7.9 192.8 %all-gather.6.cloned.1.call-start = ((), (), s32[]{:S(2)}) async-start(), calls=%async_computation.4 | async-start | bytes 14417920 | tf_op jit(solution)/shard_map/all_gather | solution.py:41
  8.7 235.2 %all-gather.10.cloned.1.call-start = ((), (), s32[]{:S(2)}) async-start(), calls=%async_computation.6 | async-start | bytes 14417920 | tf_op jit(solution)/shard_map/all_gather | solution.py:43
  9.4 446.3 %all-gather.12.cloned.1.call-start = ((), (), s32[]{:S(2)}) async-start(), calls=%async_computation.7 | async-start | bytes 31457280 | tf_op jit(solution)/shard_map/all_gather | solution.py:44
  20.2 0.7 copy-start.8
  20.2 6.9 copy-start.1
  33.3 17.2 %copy-start.9 = (f32[2048]{0:T(1024)S(1)}, f32[2048]{0:T(1024)}, u32[]{:S(2)}) copy-start(f32[2048]{0:T(1024)} %param.18) | copy-start | bytes 24580
  243.9 5.3 copy-start.13
  275.8 6.6 copy-start.10
  275.8 6.8 copy-start.11
  275.8 121.8 %all-to-all-start.1 = ((bf16[8,160,2048]{2,1,0:T(8,128)(2,1)}), bf16[8,160,2048]{2,1,0:T(8,128)(2,1)}, u32[]{:S(2)}, u32[]{:S(2)}) async-start(bf16[8,160,2048]{2,1,0:T(8,128)(2,1)} %bitcast.200), calls=%async_computation.1 | async-start | bytes 10485760 | tf_op jit(solution)/shard_map/all_to_all | solution.py:77
  444.1 6.0 copy-start.2
  450.1 5.7 copy-start.12
  482.3 8.3 copy-start.4
  510.7 142.5 %all-to-all-start.2 = ((bf16[3,32,256,128]{3,2,0,1:T(8,128)(2,1)}), bf16[3,32,256,128]{3,2,0,1:T(8,128)(2,1)}, u32[]{:S(2)}, u32[]{:S(2)}) async-start(bf16[3,32,256,128]{3,2,0,1:T(8,128)(2,1)} %pad_maximum_fusion), calls=%async_computation.2 | async-start | bytes 12582912 | tf_op jit(solution)/shard_map/all_to_all | solution.py:95
  515.6 352.6 %all-gather.14.cloned.1.call-start = ((), (), s32[]{:S(2)}) async-start(), calls=%async_computation.8 | async-start | bytes 10485760 | tf_op jit(solution)/shard_map/all_gather | solution.py:46
  868.2 6.8 copy-start.6
  868.3 6.7 copy-start.7
  871.9 4.4 copy-start.5
  875.0 1.6 copy-start.3
Sparse Core Ops, SparseCore 0:
  9.5 78.8 all-gather.7
  90.0 76.1 all-gather.5
  167.7 76.1 all-gather.9
  245.3 154.8 all-gather.11
  517.7 59.0 all-gather.13
where the time goes:
time: 918 us; the launch traced here: 909 us
  waiting for transfers between devices  276 us (30%)
  matrix products  204 us (22%)
  blocking collectives  181 us (20%)
  local copies, waits for them, and re-layouts  113 us (12%)
  other arithmetic  110 us (12%)
  between operations  14.4 us (2%)
  starting transfers between devices  10.9 us (1%)
    all_to_all x1, waiting for transfers between devices, local(): lax.all_to_all(grouped, 'expert', split_axis=1, concat_axis=2, tiled=True)  137 us
    all_to_all x1, blocking collectives, local(): lax.all_to_all(outgoing, 'expert', split_axis=0, concat_axis=0, tiled=True)  123 us
    all_to_all x1, waiting for transfers between devices, local(): lax.all_to_all(results, 'expert', split_axis=0, concat_axis=0, tiled=True)  110 us
    dot_general x4, matrix products, attend(): jnp.einsum('pqk,pke->pqe', probs, value_rows, preferred_element_type=jnp....  58.9 us
    sub x4, other arithmetic, attend(): scores = scores - jnp.max(scores, axis=-1, keepdims=True)  56.5 us
    all_to_all x1, blocking collectives, local(): lax.all_to_all(attended, 'expert', split_axis=1, concat_axis=0, tiled=True)  52.2 us
    dot_general x4, matrix products, attend(): jnp.einsum('pqe,pke->pqk', query_block, key_rows, preferred_element_type=...  36.5 us
    dot_general x4, matrix products, local(): jnp.einsum('sjcf,jfd->sjcd', hidden[..., low:low + ff_part], down_full[:,...  29 us
  transfers between devices with their start and end apart: 7, of which 3 were waited for; matrix products, arithmetic and copies ran while one was open for 37% of the time, Pallas kernels for 0%

commit v1 on v0

--- a/solution.py
+++ b/solution.py
@@ -2,6 +2,25 @@
 import jax.numpy as jnp
 from jax import lax
 from jax.sharding import PartitionSpec as P
+
+
+def gather_around(value, axis, dim):
+    size, mine, rows = (lax.axis_size(axis), lax.axis_index(axis), value.shape[dim])
+    right = [(i, (i + 1) % size) for i in range(size)]
+    downward = [(i, (i - 1) % size) for i in range(size)]
+    out = jnp.zeros((*value.shape[:dim], size * rows, *value.shape[dim + 1 :]), value.dtype)
+    out = lax.dynamic_update_slice_in_dim(out, value, mine * rows, axis=dim)
+    from_left = from_right = value
+    middle = size // 2
+    for lap in range(1, middle + 1):
+        from_left = lax.ppermute(from_left, axis, right)
+        out = lax.dynamic_update_slice_in_dim(out, from_left, (mine - lap) % size * rows, axis=dim)
+        if lap < size - middle:
+            from_right = lax.ppermute(from_right, axis, downward)
+            out = lax.dynamic_update_slice_in_dim(
+                out, from_right, (mine + lap) % size * rows, axis=dim
+            )
+    return out
 
 
 def norm_rows(values, gain):
@@ -40,7 +59,7 @@
     capacity = max(2, tok_count * 10 // (4 * expert_total))
     gate_full = lax.all_gather(expert_gate, "rep", axis=2, tiled=True)
     up_full = lax.all_gather(expert_up, "rep", axis=2, tiled=True)
-    down_full = lax.all_gather(expert_down, "rep", axis=1, tiled=True)
+    down_full = gather_around(expert_down, "rep", 1)
     qkv_full = lax.all_gather(teacher_qkv, "rep", axis=2, tiled=True)
     qk_gain_full = lax.all_gather(qk_gain, "rep", axis=1, tiled=True)
     out_full = lax.all_gather(teacher_out, "rep", axis=0, tiled=True)

time: 918 us -> 951 us (1.036)
  waiting for transfers between devices: 276 us -> 400 us
  blocking collectives: 181 us -> 57.6 us
  local copies, waits for them, and re-layouts: 113 us -> 132 us
    ppermute x0 -> x3, waiting for transfers between devices: none -> 153 us  [the longest x2 153 us: gather_around(): from_left = lax.ppermute(from_left, axis, right)]
    all_to_all x1 -> x0, blocking collectives: 123 us -> none  [local(): lax.all_to_all(outgoing, 'expert', split_axis=0, concat_axis=0, tiled=True)]
    all_gather x1 -> x0, waiting for transfers between devices: 26.6 us -> none  [local(): down_full = lax.all_gather(expert_down, 'rep', axis=1, tiled=True)]
    dynamic_update_slice x0 -> x4, local copies, waits for them, and re-layouts: none -> 14.2 us  [the longest x2 8.58 us: gather_around(): lax.dynamic_update_slice_in_dim(out, from_left, (mine - lap) % size * row...]
  transfers between devices with their start and end apart: 7 -> 10, of which waited for: 3 -> 4; matrix products, arithmetic and copies ran while one was open for 37% -> 38% of each run, Pallas kernels for 0% -> 0%
where the time goes in v1:
time: 951 us; the launch traced here: 943 us
  waiting for transfers between devices  400 us (42%)
  matrix products  204 us (21%)
  local copies, waits for them, and re-layouts  132 us (14%)
  other arithmetic  114 us (12%)
  blocking collectives  57.6 us (6%)
  starting transfers between devices  20.4 us (2%)
  between operations  14.5 us (2%)
    ppermute x2, waiting for transfers between devices, gather_around(): from_left = lax.ppermute(from_left, axis, right)  153 us
    all_to_all x1, waiting for transfers between devices, local(): lax.all_to_all(grouped, 'expert', split_axis=1, concat_axis=2, tiled=True)  136 us
    all_to_all x1, waiting for transfers between devices, local(): lax.all_to_all(results, 'expert', split_axis=0, concat_axis=0, tiled=True)  109 us
    dot_general x4, matrix products, attend(): jnp.einsum('pqk,pke->pqe', probs, value_rows, preferred_element_type=jnp....  58.9 us
    sub x4, other arithmetic, attend(): scores = scores - jnp.max(scores, axis=-1, keepdims=True)  58.3 us
    all_to_all x1, blocking collectives, local(): lax.all_to_all(attended, 'expert', split_axis=1, concat_axis=0, tiled=True)  52.2 us
    dot_general x4, matrix products, attend(): jnp.einsum('pqe,pke->pqk', query_block, key_rows, preferred_element_type=...  36.8 us
    dot_general x4, matrix products, local(): jnp.einsum('sjcf,jfd->sjcd', hidden[..., low:low + ff_part], down_full[:,...  27.8 us
  transfers between devices with their start and end apart: 10, of which 4 were waited for; matrix products, arithmetic and copies ran while one was open for 38% of the time, Pallas kernels for 0%

profile of v1, /device:TPU:0, one launch (start us, length us, event | category | flops | bytes accessed | tf_op | source)
XLA Modules:
  0.0 942.6 jit_solution(1703464063962287516)
XLA Ops:
  8.7 10.7 %copy.124 = bf16[2048,3,4,128]{0,3,2,1:T(8,128)(2,1)} copy(bf16[2048,3,4,128]{3,2,1,0:T(4,128)(2,1)} %param.23) | data formatting | bytes 12582912 | tf_op args[8]
  73.4 108.6 %collective-permute-done = bf16[2,352,2048]{2,1,0:T(8,128)(2,1)} collective-permute-done((bf16[2,352,2048]{2,1,0:T(8,128)(2,1)S(1)}, bf16[2,352,2048]{2,1,0:T(8,128)(2,1)}, u32[]{:S(2)}, u32[]{:S(2)}) %collective-permute-start) | collective-permute-done | bytes 2883616 | tf_op jit(solution)/shard_map/ppermute | solution.py:16
  197.1 44.0 %collective-permute-done.2 = bf16[2,352,2048]{2,1,0:T(8,128)(2,1)} collective-permute-done((bf16[2,352,2048]{2,1,0:T(8,128)(2,1)}, bf16[2,352,2048]{2,1,0:T(8,128)(2,1)}, u32[]{:S(2)}, u32[]{:S(2)}) %collective-permute-start.2) | collective-permute-done | bytes 2883616 | tf_op jit(solution)/shard_map/ppermute | solution.py:16
  245.9 15.8 %fusion.23 = f32[2,8,80,1408]{3,2,1,0:T(8,128)} fusion(bf16[2,2048,1408]{1,2,0:T(8,128)(2,1)} %all-gather.7.cloned.1.call-done, bf16[8,2,80,2048]{3,2,1,0:T(8,128)(2,1)} %bitcast.10), kind=kOutput, calls=%fused_computation.23 | convolution fusion | flops 7381975040 | bytes 23986176 | tf_op jit(solution)/shard_map/sjcd,jdf->sjcf/dot_general | solution.py:82
  261.7 16.4 %fusion.27 = bf16[8,2,80,1408]{3,2,0,1:T(8,128)(2,1)} fusion(f32[2,8,80,1408]{3,2,1,0:T(8,128)} %fusion.23, bf16[2,2048,1408]{1,2,0:T(8,128)(2,1)} %all-gather.5.cloned.1.call-done, bf16[8,2,80,2048]{3,2,1,0:T(8,128)(2,1)} %bitcast.10), kind=kOutput, calls=%fused_computation.31 | convolution fusion | flops 7392788480 | bytes 27590656 | tf_op jit(solution)/shard_map/sjcd,jdf->sjcf/dot_general | solution.py:81
  296.8 9.2 fusion.31
  320.9 108.9 %all-to-all-done.1 = bf16[8,160,2048]{2,1,0:T(8,128)(2,1)} async-done(((bf16[8,160,2048]{2,1,0:T(8,128)(2,1)}), bf16[8,160,2048]{2,1,0:T(8,128)(2,1)}, u32[]{:S(2)}, u32[]{:S(2)}) %all-to-all-start.1) | async-done | bytes 5242912 | tf_op jit(solution)/shard_map/all_to_all | solution.py:96
  429.8 12.2 %gather_fusion.1 = bf16[1024,2048]{1,0:T(8,128)(2,1)} fusion(bf16[1280,2048]{1,0:T(8,128)(2,1)} %bitcast.25, s32[1024]{0:T(1024)S(1)} %broadcast_clamp_fusion), kind=kCustom, calls=%fused_computation.1 | custom fusion | bytes 8392704 | tf_op jit(solution)/shard_map/jit(_take)/gather | solution.py:99
  449.6 20.7 %multiply_reduce_fusion.1 = f32[512,2048]{1,0:T(8,128)} fusion(bf16[512,2,2048]{2,1,0:T(2,128)(2,1)} %gather.15, pred[512,2]{1,0:T(8,128)(4,1)S(1)} %copy.113, f32[512,2]{1,0:T(8,128)S(1)} %bitcast.213), kind=kLoop, calls=%fused_computation.28 | loop fusion | flops 7340032 | bytes 8393728 | tf_op jit(solution)/shard_map/reduce_sum | solution.py:100
  487.8 26.4 %fusion.36 = f32[3,2,16,256,128]{3,4,2,0,1:T(8,128)} fusion(bf16[2048,3,16,128]{0,3,2,1:T(8,128)(2,1)} %all-gather.9.cloned.1.call-done, f32[2048]{0:T(1024)S(1)} %copy-done.13, f32[256,2]{0,1:T(2,128)S(1)} %add_rsqrt_fusion.2, f32[256,2,2048]{2,1,0:T(2,128)} %reduce_sum.76, bf16[1,256,2,2048]{3,2,1,0:T(2,128)(2,1)S(1)} %copy-done.2), kind=kOutput, calls=%fused_computation.44 | convolution fusion | flops 12892241920 | bytes 44050432 | tf_op jit(solution)/shard_map/sid,djhe->jihse/dot_general | solution.py:106
  548.3 136.4 %all-to-all-done.2 = bf16[3,32,256,128]{3,2,0,1:T(8,128)(2,1)} async-done(((bf16[3,32,256,128]{3,2,0,1:T(8,128)(2,1)}), bf16[3,32,256,128]{3,2,0,1:T(8,128)(2,1)}, u32[]{:S(2)}, u32[]{:S(2)}) %all-to-all-start.2) | async-done | bytes 6291488 | tf_op jit(solution)/shard_map/all_to_all | solution.py:114
  691.6 154.0 %while.10 = (s32[]{:T(128)}, bf16[4,4,512,128]{3,2,0,1:T(8,128)(2,1)}, bf16[4,4,512,128]{3,2,0,1:T(8,128)(2,1)}, bf16[4,2048,128]{2,1,0:T(8,128)(2,1)S(1)}, bf16[4,2048,128]{2,1,0:T(8,128)(2,1)}, /*index=5*/s32[]{:T(128)}) while((s32[]{:T(128)}, bf16[4,4,512,128]{3,2,0,1:T(8,128)(2,1)}, bf16[4,4,512,128]{3,2,0,1:T(8,128)(2,1)}, ...), condition=%wide.region_13.14_spmd, body=%wide.region_10.13_spmd.sunk | while | flops 2185500672 | bytes 72369224 | solution.py:137
  700.8 14.6 %fusion.111 = f32[4,512]{1,0:T(4,128)S(1)} fusion(f32[4,512,2048]{2,1,0:T(8,128)} %fusion.110), kind=kOutput, calls=%fused_computation.139.clone.1 | output fusion | flops 16779264 | bytes 16785408 | tf_op jit(solution)/shard_map/while/body/eval_jaxpr/sub | solution.py:126
  715.4 14.7 %fusion.112 = bf16[4,4,512,128]{3,2,0,1:T(8,128)(2,1)} fusion(bf16[4,4,512,128]{3,2,0,1:T(8,128)(2,1)} %get-tuple-element.119, s32[]{:T(128)} %get-tuple-element.118, bf16[4,2048,128]{2,1,0:T(8,128)(2,1)} %get-tuple-element.128, f32[4,512]{1,0:T(4,128)S(1)} %fusion.111, f32[4,512,2048]{2,1,0:T(8,128)} %fusion.110), kind=kOutput, calls=%fused_computation.13.clone.1 | convolution fusion | flops 1094979584 | bytes 36184576 | tf_op jit(solution)/shard_map/while/body/eval_jaxpr/pqk,pke->pqe/dot_general | solution.py:129
  730.1 9.2 fusion.110
  739.3 14.6 %fusion.111 = f32[4,512]{1,0:T(4,128)S(1)} fusion(f32[4,512,2048]{2,1,0:T(8,128)} %fusion.110), kind=kOutput, calls=%fused_computation.139.clone.1 | output fusion | flops 16779264 | bytes 16785408 | tf_op jit(solution)/shard_map/while/body/eval_jaxpr/sub | solution.py:126
  753.9 14.7 %fusion.112 = bf16[4,4,512,128]{3,2,0,1:T(8,128)(2,1)} fusion(bf16[4,4,512,128]{3,2,0,1:T(8,128)(2,1)} %get-tuple-element.119, s32[]{:T(128)} %get-tuple-element.118, bf16[4,2048,128]{2,1,0:T(8,128)(2,1)} %get-tuple-element.128, f32[4,512]{1,0:T(4,128)S(1)} %fusion.111, f32[4,512,2048]{2,1,0:T(8,128)} %fusion.110), kind=kOutput, calls=%fused_computation.13.clone.1 | convolution fusion | flops 1094979584 | bytes 36184576 | tf_op jit(solution)/shard_map/while/body/eval_jaxpr/pqk,pke->pqe/dot_general | solution.py:129
  768.7 9.2 fusion.110
  777.9 14.6 %fusion.111 = f32[4,512]{1,0:T(4,128)S(1)} fusion(f32[4,512,2048]{2,1,0:T(8,128)} %fusion.110), kind=kOutput, calls=%fused_computation.139.clone.1 | output fusion | flops 16779264 | bytes 16785408 | tf_op jit(solution)/shard_map/while/body/eval_jaxpr/sub | solution.py:126
  792.4 14.7 %fusion.112 = bf16[4,4,512,128]{3,2,0,1:T(8,128)(2,1)} fusion(bf16[4,4,512,128]{3,2,0,1:T(8,128)(2,1)} %get-tuple-element.119, s32[]{:T(128)} %get-tuple-element.118, bf16[4,2048,128]{2,1,0:T(8,128)(2,1)} %get-tuple-element.128, f32[4,512]{1,0:T(4,128)S(1)} %fusion.111, f32[4,512,2048]{2,1,0:T(8,128)} %fusion.110), kind=kOutput, calls=%fused_computation.13.clone.1 | convolution fusion | flops 1094979584 | bytes 36184576 | tf_op jit(solution)/shard_map/while/body/eval_jaxpr/pqk,pke->pqe/dot_general | solution.py:129
  807.2 9.2 fusion.110
  816.4 14.6 %fusion.111 = f32[4,512]{1,0:T(4,128)S(1)} fusion(f32[4,512,2048]{2,1,0:T(8,128)} %fusion.110), kind=kOutput, calls=%fused_computation.139.clone.1 | output fusion | flops 16779264 | bytes 16785408 | tf_op jit(solution)/shard_map/while/body/eval_jaxpr/sub | solution.py:126
  830.9 14.7 %fusion.112 = bf16[4,4,512,128]{3,2,0,1:T(8,128)(2,1)} fusion(bf16[4,4,512,128]{3,2,0,1:T(8,128)(2,1)} %get-tuple-element.119, s32[]{:T(128)} %get-tuple-element.118, bf16[4,2048,128]{2,1,0:T(8,128)(2,1)} %get-tuple-element.128, f32[4,512]{1,0:T(4,128)S(1)} %fusion.111, f32[4,512,2048]{2,1,0:T(8,128)} %fusion.110), kind=kOutput, calls=%fused_computation.13.clone.1 | convolution fusion | flops 1094979584 | bytes 36184576 | tf_op jit(solution)/shard_map/while/body/eval_jaxpr/pqk,pke->pqe/dot_general | solution.py:129
  849.1 52.2 %all_to_all.40 = bf16[4,2048,128]{2,0,1:T(4,128)(2,1)S(1)} all-to-all(bf16[4,2048,128]{2,0,1:T(4,128)(2,1)S(1)} %copy.135), channel_id=1, replica_groups=mesh['expert'=8,'rep'=4] {'expert'}, dimensions={1} | all-to-all | bytes 4194304 | tf_op jit(solution)/shard_map/all_to_all | solution.py:139
  (139 shorter events, 221.7 us)
Async XLA Ops:
  7.2 921.9 %copy-start = (f32[1024]{0:T(1024)S(1)}, f32[1024]{0:T(1024)}, u32[]{:S(2)}) copy-start(f32[1024]{0:T(1024)} %param.27) | copy-start | bytes 12292
  7.2 238.7 %all-gather.7.cloned.1.call-start = ((), (), s32[]{:S(2)}) async-start(), calls=%async_computation.5 | async-start | bytes 14417920 | tf_op jit(solution)/shard_map/all_gather | solution.py:61
  7.9 253.8 %all-gather.5.cloned.1.call-start = ((), (), s32[]{:S(2)}) async-start(), calls=%async_computation.4 | async-start | bytes 14417920 | tf_op jit(solution)/shard_map/all_gather | solution.py:60
  8.7 479.1 %all-gather.9.cloned.1.call-start = ((), (), s32[]{:S(2)}) async-start(), calls=%async_computation.6 | async-start | bytes 31457280 | tf_op jit(solution)/shard_map/all_gather | solution.py:63
  19.4 6.9 copy-start.1
  32.5 16.7 %copy-start.10 = (f32[2048]{0:T(1024)S(1)}, f32[2048]{0:T(1024)}, u32[]{:S(2)}) copy-start(f32[2048]{0:T(1024)} %param.18) | copy-start | bytes 24580
  64.0 7.6 copy-start.7
  64.0 181.9 %all-to-all-start = ((bf16[8,160,2048]{2,1,0:T(8,128)(2,1)}), bf16[8,160,2048]{2,1,0:T(8,128)(2,1)}, u32[]{:S(2)}, u32[]{:S(2)}) async-start(bf16[8,160,2048]{2,1,0:T(8,128)(2,1)} %select_select_fusion), calls=%async_computation | async-start | bytes 10485760 | tf_op jit(solution)/shard_map/all_to_all | solution.py:79
  71.6 110.4 %collective-permute-start = (bf16[2,352,2048]{2,1,0:T(8,128)(2,1)S(1)}, bf16[2,352,2048]{2,1,0:T(8,128)(2,1)}, u32[]{:S(2)}, u32[]{:S(2)}) collective-permute-start(bf16[2,352,2048]{2,1,0:T(8,128)(2,1)S(1)} %copy-done.7), channel_id=1, source_target_pairs={{0,1},{1,2},{2,3},{3,0},{4,5},{5,6},{6,7},{7,4},{8,9},{9,10},{10,1... | collective-permute-start | bytes 8650760 | tf_op jit(solution)/shard_map/ppermute | solution.py:16
  71.7 121.7 %collective-permute-start.1 = (bf16[2,352,2048]{2,1,0:T(8,128)(2,1)S(1)}, bf16[2,352,2048]{2,1,0:T(8,128)(2,1)}, u32[]{:S(2)}, u32[]{:S(2)}) collective-permute-start(bf16[2,352,2048]{2,1,0:T(8,128)(2,1)S(1)} %copy-done.7), channel_id=1, source_target_pairs={{0,3},{1,0},{2,1},{3,2},{4,7},{5,4},{6,5},{7,6},{8,11},{9,8},{10,9... | collective-permute-start | bytes 8650760 | tf_op jit(solution)/shard_map/ppermute | solution.py:19
  182.0 59.1 %collective-permute-start.2 = (bf16[2,352,2048]{2,1,0:T(8,128)(2,1)}, bf16[2,352,2048]{2,1,0:T(8,128)(2,1)}, u32[]{:S(2)}, u32[]{:S(2)}) collective-permute-start(bf16[2,352,2048]{2,1,0:T(8,128)(2,1)} %collective-permute-done), channel_id=1, source_target_pairs={{0,1},{1,2},{2,3},{3,0},{4,5},{5,6},{6,7},{7,4},{8,9},{9,10},{10,1... | collective-permute-start | bytes 8650760 | tf_op jit(solution)/shard_map/ppermute | solution.py:16
  278.1 5.3 copy-start.14
  308.7 6.5 copy-start.11
  308.7 6.7 copy-start.12
  308.7 121.1 %all-to-all-start.1 = ((bf16[8,160,2048]{2,1,0:T(8,128)(2,1)}), bf16[8,160,2048]{2,1,0:T(8,128)(2,1)}, u32[]{:S(2)}, u32[]{:S(2)}) async-start(bf16[8,160,2048]{2,1,0:T(8,128)(2,1)} %bitcast.200), calls=%async_computation.1 | async-start | bytes 10485760 | tf_op jit(solution)/shard_map/all_to_all | solution.py:96
  476.1 6.0 copy-start.2
  482.2 5.7 copy-start.13
  514.2 8.3 copy-start.4
  542.6 142.1 %all-to-all-start.2 = ((bf16[3,32,256,128]{3,2,0,1:T(8,128)(2,1)}), bf16[3,32,256,128]{3,2,0,1:T(8,128)(2,1)}, u32[]{:S(2)}, u32[]{:S(2)}) async-start(bf16[3,32,256,128]{3,2,0,1:T(8,128)(2,1)} %pad_maximum_fusion), calls=%async_computation.2 | async-start | bytes 12582912 | tf_op jit(solution)/shard_map/all_to_all | solution.py:114
  547.7 354.1 %all-gather.11.cloned.1.call-start = ((), (), s32[]{:S(2)}) async-start(), calls=%async_computation.7 | async-start | bytes 10485760 | tf_op jit(solution)/shard_map/all_gather | solution.py:65
  901.8 6.8 copy-start.6
  901.8 6.7 copy-start.8
  905.5 4.4 copy-start.5
  908.5 1.6 copy-start.3
  (1 other events, 0.7 us)
Sparse Core Ops, SparseCore 0:
  9.5 90.3 all-gather.6
  101.5 122.8 all-gather.4
  226.0 154.8 all-gather.8
  549.8 59.4 all-gather.10
